TPU v7x, 32 devices: a whole 2x2x4 slice. The times are simulated.
32 devices in a mesh: gx: 4 (over z), gy: 2 (over y), gz: 4 (over x, core).
Axes of the slice: x: 2, y: 2, z: 4, core: 2. Of those that a mesh axis runs over, the one named last changes fastest.
Arguments:
- positions: float32 [3, 4, 2, 8, 128], P(None, 'gx', 'gy', 'gz'), may hold values from 0 to 8, as said below
- velocity: float32 [3, 4, 2, 8, 128], P(None, 'gx', 'gy', 'gz'), may hold values from -16 to 16
- counts: int32 [4, 2, 8], P('gx', 'gy', 'gz'), may hold values from 0 to 128, as said below
Outputs:
- velocity_new: float32 [3, 4, 2, 8, 128], P(None, 'gx', 'gy', 'gz')
- pressure: float32 [4, 2, 8, 128], P('gx', 'gy', 'gz')
Inputs may be any that keep to these rules, and one draw needn't show every extreme that they name: `positions`: component k of the position of any slot of tile (a, b, c) lies in [t, t + 1), where t is a, b or c for k = 0, 1, 2. A tile's particles fill its first counts[a, b, c] slots. In every column of tiles the bottom tile is full, the tiles below one topmost wet tile hold 96 or more particles, and the tiles above it are empty.
All inputs are finite; a program needn't handle non-finite values.
Results may differ from a plain program's by a relative error of at most 0.0003.
Values sent between devices are 32-bit elements; how exact they have to be, the bound alone decides.
No kernel may reach another device: no remote copies, remote signals or barrier semaphores. Data moves between devices by JAX's collectives and lax.ppermute only.
A program may use at most 64 MiB of HBM per device.

v0:
```python
import jax
import jax.numpy as jnp
from jax import lax
from jax.sharding import PartitionSpec as P

ITERS = 3
DIAG_SHIFT = 0.05
VISCOSITY = 0.5
GRAVITY = 0.1
GRADIENT_GAIN = 32.0
AXES = (("gx", 1), ("gy", 2), ("gz", 3))


def with_halo(cells, sides, width):
    for axis, dim in sides:
        count = lax.axis_size(axis)
        ends = count - 1
        head = lax.slice_in_dim(cells, 0, width, axis=dim)
        tail = lax.slice_in_dim(cells, cells.shape[dim] - width, cells.shape[dim], axis=dim)
        cells = jnp.concatenate(
            [
                lax.ppermute(tail, axis, [(i, (i + 1) % count) for i in range(ends)]),
                cells,
                lax.ppermute(head, axis, [((i + 1) % count, i) for i in range(ends)]),
            ],
            axis=dim,
        )
    return cells


def neighbours(rim):
    comps, size_x, size_y, size_z, width = rim.shape
    blocks = []
    for ax in range(size_x - 2):
        for ay in range(size_y - 2):
            for az in range(size_z - 2):
                window = rim[:, ax : ax + 3, ay : ay + 3, az : az + 3, :]
                blocks.append(window.reshape(comps, 27 * width))
    return jnp.stack(blocks, axis=1)


def flat(cells):
    return cells.reshape(cells.shape[0], -1, cells.shape[4])


def wsum(weight, near):
    return jnp.sum(weight[None] * near[:, :, None, :], axis=-1)


def tile_corners(block_shape):
    _, size_x, size_y, size_z, _ = block_shape
    base = (
        lax.axis_index("gx") * size_x,
        lax.axis_index("gy") * size_y,
        lax.axis_index("gz") * size_z,
    )
    corners = []
    for ax in range(size_x):
        for ay in range(size_y):
            for az in range(size_z):
                corners.append(jnp.stack([base[0] + ax, base[1] + ay, base[2] + az]))
    return jnp.stack(corners, axis=1).astype(jnp.float32)


def on_device(positions, velocity, counts):
    block_shape = positions.shape
    width = positions.shape[4]
    slot_ids = jnp.arange(width, dtype=jnp.int32)
    valid_mask = (slot_ids[None, None, None, :] < counts[:, :, :, None]).astype(jnp.float32)[None]
    packed = jnp.concatenate([positions, valid_mask, velocity], axis=0)
    near_all = neighbours(with_halo(packed, AXES, 1))
    near_x = near_all[0:3]
    near_valid = near_all[3]
    near_v = near_all[4:7]
    own_x = flat(positions)
    own_valid = flat(valid_mask)[0]
    own_v = flat(velocity)
    offset = own_x[:, :, :, None] - near_x[:, :, None, :]
    distance = offset[0] * offset[0] + offset[1] * offset[1] + offset[2] * offset[2]
    closeness = jnp.maximum(1.0 - distance, 0.0)
    weight = closeness * closeness * own_valid[:, :, None] * near_valid[:, None, :]
    corner = tile_corners(block_shape)[:, :, None]
    local_own = own_x - corner
    local_near = near_x - corner
    row = jnp.sum(weight, axis=-1)[None]
    sums = wsum(weight, jnp.concatenate([near_v, local_near], axis=0))
    near_sums = sums[0:3]
    lever = local_own * row - sums[3:6]
    gravity_pull = jnp.array([0.0, 0.0, -GRAVITY], jnp.float32).reshape(3, 1, 1)
    predicted = own_valid[None] * (
        own_v + VISCOSITY / width * (near_sums - row * own_v) + gravity_pull
    )
    diagonal = DIAG_SHIFT + row / width

    def shaped(values):
        return values.reshape(values.shape[0], *block_shape[1:])

    near_pred = neighbours(with_halo(shaped(predicted), AXES, 1))
    dotted = jnp.sum(near_pred * local_near, axis=0, keepdims=True)
    psums = wsum(weight, jnp.concatenate([near_pred, dotted], axis=0))
    flux = jnp.sum(local_own * psums[0:3], axis=0, keepdims=True) - psums[3:4]
    source = -(GRADIENT_GAIN / width) * (jnp.sum(predicted * lever, axis=0, keepdims=True) - flux)

    def operate(field):
        near_field = neighbours(with_halo(shaped(field), AXES, 1))
        return (near_field, diagonal * field - wsum(weight, near_field) / width)

    def paired_sums(residual, precond, applied):
        pair = jnp.stack([jnp.sum(residual * precond), jnp.sum(precond * applied)])
        total = lax.psum(pair, ("gx", "gy", "gz"))
        return (total[0], total[1])

    pressure = jnp.zeros_like(source)
    residual = source
    precond = residual / diagonal
    near_dir, applied = operate(precond)
    norm_now, curvature_sum = paired_sums(residual, precond, applied)
    step_size = norm_now / curvature_sum
    direction = precond
    along = applied
    near_pressure = jnp.zeros_like(near_dir)
    for iteration in range(ITERS):
        pressure = pressure + step_size * direction
        near_pressure = near_pressure + step_size * near_dir
        residual = residual - step_size * along
        if iteration + 1 < ITERS:
            precond = residual / diagonal
            near_fresh, applied = operate(precond)
            norm_next, curvature_sum = paired_sums(residual, precond, applied)
            blend = norm_next / norm_now
            step_size = norm_next / (curvature_sum - blend * norm_next / step_size)
            direction = precond + blend * direction
            near_dir = near_fresh + blend * near_dir
            along = applied + blend * along
            norm_now = norm_next
    grads = wsum(weight, jnp.concatenate([near_pressure, near_pressure * local_near], axis=0))
    moments = local_own * grads[0:1] - grads[1:4]
    velocity_new = predicted - GRADIENT_GAIN / width * (pressure * lever - moments)
    return (shaped(velocity_new), shaped(pressure)[0])


def solution(mesh):
    in_specs = (
        P(None, "gx", "gy", "gz", None),
        P(None, "gx", "gy", "gz", None),
        P("gx", "gy", "gz"),
    )
    out_specs = (P(None, "gx", "gy", "gz", None), P("gx", "gy", "gz", None))
    return jax.shard_map(
        on_device, mesh=mesh, in_specs=in_specs, out_specs=out_specs, check_vma=False
    )
```

profile of v0, /device:TPU:0, one launch (start us, length us, event | category | flops | bytes accessed | tf_op | source)
XLA Modules:
  0.0 319.3 jit_solution(7614055411883678423)
XLA Ops:
  4.0 5.6 %collective-permute-start = (f32[7,1,1,2,128]{4,0,3,2,1:T(8,128)S(1)}, f32[7,1,1,2,128]{4,0,3,2,1:T(8,128)S(1)}, u32[]{:S(2)}, u32[]{:S(2)}) collective-permute-start(f32[7,1,1,2,128]{4,0,3,2,1:T(8,128)S(1)} %pad_maximum_fusion.19), channel_id=1, source_target_pairs={{0,8},{8,16},{16,24},{1,9},{9,17},{17,25},{2,10},{10,18},{18,26},{... | collective-permute-start | bytes 21512 | tf_op jit(solution)/shard_map/ppermute | solution.py:22
  12.3 4.5 %collective-permute-start.2 = (f32[7,3,1,2,128]{4,0,3,2,1:T(8,128)S(1)}, f32[7,3,1,2,128]{4,0,3,2,1:T(8,128)S(1)}, u32[]{:S(2)}, u32[]{:S(2)}) collective-permute-start(f32[7,3,1,2,128]{4,0,3,2,1:T(8,128)S(1)} %pad_maximum_fusion.11), channel_id=1, source_target_pairs={{0,4},{1,5},{2,6},{3,7},{8,12},{9,13},{10,14},{11,15},{16,20},{17,... | collective-permute-start | bytes 64520 | tf_op jit(solution)/shard_map/ppermute | solution.py:22
  16.9 1.4 collective-permute-done.2
  21.0 3.9 %collective-permute-done.5 = f32[7,3,3,1,128]{4,0,3,2,1:T(8,128)S(1)} collective-permute-done((f32[7,3,3,1,128]{4,0,3,2,1:T(8,128)S(1)}, f32[7,3,3,1,128]{4,0,3,2,1:T(8,128)S(1)}, u32[]{:S(2)}, u32[]{:S(2)}) %collective-permute-start.5) | collective-permute-done | bytes 32288 | tf_op jit(solution)/shard_map/ppermute | solution.py:24
  25.7 1.5 broadcast_subtract_fusion
  27.2 1.6 fusion.6
  29.3 1.7 copy-done
  31.0 1.8 multiply_reduce_fusion
  34.2 4.8 %collective-permute-start.6 = (f32[3,1,1,2,128]{4,3,0,2,1:T(2,128)S(1)}, f32[3,1,1,2,128]{4,3,0,2,1:T(2,128)S(1)}, u32[]{:S(2)}, u32[]{:S(2)}) collective-permute-start(f32[3,1,1,2,128]{4,3,0,2,1:T(2,128)S(1)} %bitcast.144), channel_id=1, source_target_pairs={{0,8},{8,16},{16,24},{1,9},{9,17},{17,25},{2,10},{10,18},{18,26},{... | collective-permute-start | bytes 9224 | tf_op jit(solution)/shard_map/ppermute | solution.py:22
  41.7 4.5 %collective-permute-start.8 = (f32[3,3,1,2,128]{4,3,0,2,1:T(2,128)S(1)}, f32[3,3,1,2,128]{4,3,0,2,1:T(2,128)S(1)}, u32[]{:S(2)}, u32[]{:S(2)}) collective-permute-start(f32[3,3,1,2,128]{4,3,0,2,1:T(2,128)S(1)} %pad_maximum_fusion.15), channel_id=1, source_target_pairs={{0,4},{1,5},{2,6},{3,7},{8,12},{9,13},{10,14},{11,15},{16,20},{17,... | collective-permute-start | bytes 27656 | tf_op jit(solution)/shard_map/ppermute | solution.py:22
  49.5 3.8 %collective-permute-start.10 = (f32[3,3,3,1,128]{4,3,0,2,1:T(1,128)}, f32[3,3,3,1,128]{4,3,0,2,1:T(1,128)}, u32[]{:S(2)}, u32[]{:S(2)}) collective-permute-start(f32[3,3,3,1,128]{4,3,0,2,1:T(1,128)} %get-tuple-element.28), channel_id=1, source_target_pairs={{0,1},{1,2},{2,3},{4,5},{5,6},{6,7},{8,9},{9,10},{10,11},{12,13},{... | collective-permute-start | bytes 41480 | tf_op jit(solution)/shard_map/ppermute | solution.py:22
  53.4 1.3 copy.31
  54.7 1.5 pad_maximum_fusion.5
  56.8 1.5 stack_reshape.32
  58.3 1.4 constant_dynamic-update-slice_fusion.1
  59.7 1.4 copy.33
  61.1 1.5 stack_reshape.33
  62.6 1.4 constant_dynamic-update-slice_fusion
  66.1 3.3 %multiply_reduce_fusion.2 = f32[4,2,128]{2,1,0:T(2,128)S(1)} fusion(f32[4,2,3456]{2,1,0:T(2,128)S(1)} %copy.34, f32[2,128,3456]{2,1,0:T(8,128)} %copy-done), kind=kLoop, calls=%fused_computation.2 | loop fusion | flops 7076864 | bytes 3653632 | tf_op jit(solution)/shard_map/reduce_sum | solution.py:47
  71.4 4.6 %collective-permute-start.12 = (f32[1,1,1,2,128]{4,3,2,1,0:T(2,128)S(1)}, f32[1,1,1,2,128]{4,3,2,1,0:T(2,128)S(1)}, u32[]{:S(2)}, u32[]{:S(2)}) collective-permute-start(f32[1,1,1,2,128]{4,3,2,1,0:T(2,128)S(1)} %bitcast.160), channel_id=1, source_target_pairs={{0,8},{8,16},{16,24},{1,9},{9,17},{17,25},{2,10},{10,18},{18,26},{... | collective-permute-start | bytes 3080 | tf_op jit(solution)/shard_map/ppermute | solution.py:22
  78.6 4.5 %collective-permute-start.14 = (f32[1,3,1,2,128]{4,3,2,1,0:T(2,128)S(1)}, f32[1,3,1,2,128]{4,3,2,1,0:T(2,128)S(1)}, u32[]{:S(2)}, u32[]{:S(2)}) collective-permute-start(f32[1,3,1,2,128]{4,3,2,1,0:T(2,128)S(1)} %pad_maximum_fusion.20), channel_id=1, source_target_pairs={{0,4},{1,5},{2,6},{3,7},{8,12},{9,13},{10,14},{11,15},{16,20},{17,... | collective-permute-start | bytes 9224 | tf_op jit(solution)/shard_map/ppermute | solution.py:22
  84.5 1.5 collective-permute-start.16
  87.3 5.3 %collective-permute-done.17 = f32[1,3,3,1,128]{4,3,2,1,0:T(1,128)S(1)} collective-permute-done((f32[1,3,3,1,128]{4,3,2,1,0:T(1,128)S(1)}, f32[1,3,3,1,128]{4,3,2,1,0:T(1,128)S(1)}, u32[]{:S(2)}, u32[]{:S(2)}) %collective-permute-start.17) | collective-permute-done | bytes 4640 | tf_op jit(solution)/shard_map/ppermute | solution.py:24
  94.0 1.3 stack_reshape.34
  96.1 1.4 multiply_reduce_fusion.5
  98.8 1.8 pad_maximum_fusion.23
  100.6 43.4 %psum.21 = f32[2]{0:T(128)} all-reduce(f32[2]{0:T(128)} %pad_maximum_fusion.23), channel_id=1, replica_groups=mesh['gx'=4,'gy'=2,'gz'=4] {'gx','gy','gz'}, use_global_device_ids=true, to_apply=%region_9.0 | all-reduce | flops 2 | bytes 16 | tf_op jit(solution)/shard_map/psum | solution.py:110
  144.0 1.3 fusion.36
  148.7 4.5 %collective-permute-start.18 = (f32[1,1,1,2,128]{4,3,2,1,0:T(2,128)S(1)}, f32[1,1,1,2,128]{4,3,2,1,0:T(2,128)S(1)}, u32[]{:S(2)}, u32[]{:S(2)}) collective-permute-start(f32[1,1,1,2,128]{4,3,2,1,0:T(2,128)S(1)} %bitcast.149), channel_id=1, source_target_pairs={{0,8},{8,16},{16,24},{1,9},{9,17},{17,25},{2,10},{10,18},{18,26},{... | collective-permute-start | bytes 3080 | tf_op jit(solution)/shard_map/ppermute | solution.py:22
  155.9 4.5 %collective-permute-start.20 = (f32[1,3,1,2,128]{4,3,2,1,0:T(2,128)S(1)}, f32[1,3,1,2,128]{4,3,2,1,0:T(2,128)S(1)}, u32[]{:S(2)}, u32[]{:S(2)}) collective-permute-start(f32[1,3,1,2,128]{4,3,2,1,0:T(2,128)S(1)} %pad_maximum_fusion.21), channel_id=1, source_target_pairs={{0,4},{1,5},{2,6},{3,7},{8,12},{9,13},{10,14},{11,15},{16,20},{17,... | collective-permute-start | bytes 9224 | tf_op jit(solution)/shard_map/ppermute | solution.py:22
  164.4 4.3 %collective-permute-done.23 = f32[1,3,3,1,128]{4,3,2,1,0:T(1,128)S(1)} collective-permute-done((f32[1,3,3,1,128]{4,3,2,1,0:T(1,128)S(1)}, f32[1,3,3,1,128]{4,3,2,1,0:T(1,128)S(1)}, u32[]{:S(2)}, u32[]{:S(2)}) %collective-permute-start.23) | collective-permute-done | bytes 4640 | tf_op jit(solution)/shard_map/ppermute | solution.py:24
  169.2 1.3 stack_reshape.37
  172.7 1.4 multiply_reduce_fusion.4
  174.2 1.4 multiply_reduce_fusion.10
  175.5 1.8 pad_maximum_fusion.24
  177.4 43.4 %psum.22 = f32[2]{0:T(128)} all-reduce(f32[2]{0:T(128)} %pad_maximum_fusion.24), channel_id=1, replica_groups=mesh['gx'=4,'gy'=2,'gz'=4] {'gx','gy','gz'}, use_global_device_ids=true, to_apply=%region_13.0 | all-reduce | flops 2 | bytes 16 | tf_op jit(solution)/shard_map/psum | solution.py:110
  229.1 4.5 %collective-permute-start.24 = (f32[1,1,1,2,128]{4,3,2,1,0:T(2,128)S(1)}, f32[1,1,1,2,128]{4,3,2,1,0:T(2,128)S(1)}, u32[]{:S(2)}, u32[]{:S(2)}) collective-permute-start(f32[1,1,1,2,128]{4,3,2,1,0:T(2,128)S(1)} %bitcast.155), channel_id=1, source_target_pairs={{0,8},{8,16},{16,24},{1,9},{9,17},{17,25},{2,10},{10,18},{18,26},{... | collective-permute-start | bytes 3080 | tf_op jit(solution)/shard_map/ppermute | solution.py:22
  236.3 4.5 %collective-permute-start.26 = (f32[1,3,1,2,128]{4,3,2,1,0:T(2,128)S(1)}, f32[1,3,1,2,128]{4,3,2,1,0:T(2,128)S(1)}, u32[]{:S(2)}, u32[]{:S(2)}) collective-permute-start(f32[1,3,1,2,128]{4,3,2,1,0:T(2,128)S(1)} %pad_maximum_fusion.22), channel_id=1, source_target_pairs={{0,4},{1,5},{2,6},{3,7},{8,12},{9,13},{10,14},{11,15},{16,20},{17,... | collective-permute-start | bytes 9224 | tf_op jit(solution)/shard_map/ppermute | solution.py:22
  242.7 1.9 collective-permute-start.28
  244.6 1.5 collective-permute-start.29
  246.1 1.3 stack.113
  247.4 1.3 stack.112
  251.5 1.4 maximum_maximum_fusion.4
  254.2 1.3 stack_reshape.39
  255.5 1.3 stack_reshape.38
  257.7 1.4 multiply_reduce_fusion.3
  262.5 45.0 %psum.23 = f32[2]{0:T(128)S(1)} all-reduce(f32[2]{0:T(128)S(1)} %pad_maximum_fusion.25), channel_id=1, replica_groups=mesh['gx'=4,'gy'=2,'gz'=4] {'gx','gy','gz'}, use_global_device_ids=true, to_apply=%region_17.0 | all-reduce | flops 2 | bytes 16 | tf_op jit(solution)/shard_map/psum | solution.py:110
  315.3 3.3 %multiply_reduce_fusion.1 = f32[4,2,128]{2,1,0:T(2,128)S(1)} fusion(f32[4,2,3456]{2,1,0:T(2,128)S(1)} %copy.41, f32[2,128,3456]{2,1,0:T(8,128)} %copy-done), kind=kLoop, calls=%fused_computation.1 | loop fusion | flops 7076864 | bytes 3653632 | tf_op jit(solution)/shard_map/reduce_sum | solution.py:47
  (182 shorter events, 62.7 us)
Async XLA Ops:
  2.7 7.6 %collective-permute-start.1 = (f32[7,1,1,2,128]{4,0,3,2,1:T(8,128)S(1)}, f32[7,1,1,2,128]{4,0,3,2,1:T(8,128)S(1)}, u32[]{:S(2)}, u32[]{:S(2)}) collective-permute-start(f32[7,1,1,2,128]{4,0,3,2,1:T(8,128)S(1)} %pad_maximum_fusion.19), channel_id=1, source_target_pairs={{8,0},{16,8},{24,16},{9,1},{17,9},{25,17},{10,2},{18,10},{26,18},{... | collective-permute-start | bytes 21512 | tf_op jit(solution)/shard_map/ppermute | solution.py:24
  4.0 6.9 %collective-permute-start = (f32[7,1,1,2,128]{4,0,3,2,1:T(8,128)S(1)}, f32[7,1,1,2,128]{4,0,3,2,1:T(8,128)S(1)}, u32[]{:S(2)}, u32[]{:S(2)}) collective-permute-start(f32[7,1,1,2,128]{4,0,3,2,1:T(8,128)S(1)} %pad_maximum_fusion.19), channel_id=1, source_target_pairs={{0,8},{8,16},{16,24},{1,9},{9,17},{17,25},{2,10},{10,18},{18,26},{... | collective-permute-start | bytes 21512 | tf_op jit(solution)/shard_map/ppermute | solution.py:22
  10.3 22.5 %copy-start.21 = (f32[2,128]{1,0:T(2,128)}, f32[2,128]{1,0:T(2,128)S(1)}, u32[]{:S(2)}) copy-start(f32[2,128]{1,0:T(2,128)S(1)} %compare_convert_fusion.1) | copy-start | bytes 3076
  11.0 5.9 %collective-permute-start.3 = (f32[7,3,1,2,128]{4,0,3,2,1:T(8,128)S(1)}, f32[7,3,1,2,128]{4,0,3,2,1:T(8,128)S(1)}, u32[]{:S(2)}, u32[]{:S(2)}) collective-permute-start(f32[7,3,1,2,128]{4,0,3,2,1:T(8,128)S(1)} %pad_maximum_fusion.11), channel_id=1, source_target_pairs={{4,0},{5,1},{6,2},{7,3},{12,8},{13,9},{14,10},{15,11},{20,16},{21,... | collective-permute-start | bytes 64520 | tf_op jit(solution)/shard_map/ppermute | solution.py:24
  12.3 6.1 %collective-permute-start.2 = (f32[7,3,1,2,128]{4,0,3,2,1:T(8,128)S(1)}, f32[7,3,1,2,128]{4,0,3,2,1:T(8,128)S(1)}, u32[]{:S(2)}, u32[]{:S(2)}) collective-permute-start(f32[7,3,1,2,128]{4,0,3,2,1:T(8,128)S(1)} %pad_maximum_fusion.11), channel_id=1, source_target_pairs={{0,4},{1,5},{2,6},{3,7},{8,12},{9,13},{10,14},{11,15},{16,20},{17,... | collective-permute-start | bytes 64520 | tf_op jit(solution)/shard_map/ppermute | solution.py:22
  18.3 2.6 collective-permute-start.4
  19.6 5.3 %collective-permute-start.5 = (f32[7,3,3,1,128]{4,0,3,2,1:T(8,128)S(1)}, f32[7,3,3,1,128]{4,0,3,2,1:T(8,128)S(1)}, u32[]{:S(2)}, u32[]{:S(2)}) collective-permute-start(f32[7,3,3,1,128]{4,0,3,2,1:T(8,128)S(1)} %get-tuple-element.24), channel_id=1, source_target_pairs={{1,0},{2,1},{3,2},{5,4},{6,5},{7,6},{9,8},{10,9},{11,10},{13,12},{... | collective-permute-start | bytes 96776 | tf_op jit(solution)/shard_map/ppermute | solution.py:24
  28.9 40.6 %copy-start.5 = (f32[2,128]{1,0:T(2,128)}, f32[2,128]{1,0:T(2,128)S(1)}, u32[]{:S(2)}) copy-start(f32[2,128]{1,0:T(2,128)S(1)} %get-tuple-element.17) | copy-start | bytes 3076
  32.8 15.4 %copy-start.12 = (f32[6,2,128]{2,1,0:T(2,128)}, f32[6,2,128]{2,1,0:T(2,128)S(1)}, u32[]{:S(2)}) copy-start(f32[6,2,128]{2,1,0:T(2,128)S(1)} %multiply_reduce_fusion) | copy-start | bytes 18436
  32.8 36.6 %copy-start.10 = (f32[3,1,1,2,128]{4,3,2,1,0:T(2,128)S(1)}, f32[3,1,1,2,128]{4,3,2,1,0:T(2,128)}, u32[]{:S(2)}) copy-start(f32[3,1,1,2,128]{4,3,2,1,0:T(2,128)} %param.4) | copy-start | bytes 9220
  32.9 60.3 %copy-start.3 = (f32[3,2,128]{2,1,0:T(2,128)}, f32[3,2,128]{2,1,0:T(2,128)S(1)}, u32[]{:S(2)}) copy-start(f32[3,2,128]{2,1,0:T(2,128)S(1)} %fusion.20) | copy-start | bytes 9220
  32.9 6.1 %collective-permute-start.7 = (f32[3,1,1,2,128]{4,3,0,2,1:T(2,128)S(1)}, f32[3,1,1,2,128]{4,3,0,2,1:T(2,128)S(1)}, u32[]{:S(2)}, u32[]{:S(2)}) collective-permute-start(f32[3,1,1,2,128]{4,3,0,2,1:T(2,128)S(1)} %bitcast.143), channel_id=1, source_target_pairs={{8,0},{16,8},{24,16},{9,1},{17,9},{25,17},{10,2},{18,10},{26,18},{... | collective-permute-start | bytes 9224 | tf_op jit(solution)/shard_map/ppermute | solution.py:24
  34.2 6.1 %collective-permute-start.6 = (f32[3,1,1,2,128]{4,3,0,2,1:T(2,128)S(1)}, f32[3,1,1,2,128]{4,3,0,2,1:T(2,128)S(1)}, u32[]{:S(2)}, u32[]{:S(2)}) collective-permute-start(f32[3,1,1,2,128]{4,3,0,2,1:T(2,128)S(1)} %bitcast.144), channel_id=1, source_target_pairs={{0,8},{8,16},{16,24},{1,9},{9,17},{17,25},{2,10},{10,18},{18,26},{... | collective-permute-start | bytes 9224 | tf_op jit(solution)/shard_map/ppermute | solution.py:22
  40.4 9.2 %copy-start.22 = (f32[3,1,1,2,128]{4,3,0,2,1:T(2,128)}, f32[3,1,1,2,128]{4,3,0,2,1:T(2,128)S(1)}, u32[]{:S(2)}) copy-start(f32[3,1,1,2,128]{4,3,0,2,1:T(2,128)S(1)} %collective-permute-done.6) | copy-start | bytes 9220
  40.4 5.9 %collective-permute-start.9 = (f32[3,3,1,2,128]{4,3,0,2,1:T(2,128)S(1)}, f32[3,3,1,2,128]{4,3,0,2,1:T(2,128)S(1)}, u32[]{:S(2)}, u32[]{:S(2)}) collective-permute-start(f32[3,3,1,2,128]{4,3,0,2,1:T(2,128)S(1)} %pad_maximum_fusion.15), channel_id=1, source_target_pairs={{4,0},{5,1},{6,2},{7,3},{12,8},{13,9},{14,10},{15,11},{20,16},{21,... | collective-permute-start | bytes 27656 | tf_op jit(solution)/shard_map/ppermute | solution.py:24
  41.7 5.9 %collective-permute-start.8 = (f32[3,3,1,2,128]{4,3,0,2,1:T(2,128)S(1)}, f32[3,3,1,2,128]{4,3,0,2,1:T(2,128)S(1)}, u32[]{:S(2)}, u32[]{:S(2)}) collective-permute-start(f32[3,3,1,2,128]{4,3,0,2,1:T(2,128)S(1)} %pad_maximum_fusion.15), channel_id=1, source_target_pairs={{0,4},{1,5},{2,6},{3,7},{8,12},{9,13},{10,14},{11,15},{16,20},{17,... | collective-permute-start | bytes 27656 | tf_op jit(solution)/shard_map/ppermute | solution.py:22
  48.2 6.5 %collective-permute-start.11 = (f32[3,3,3,1,128]{4,3,0,2,1:T(1,128)}, f32[3,3,3,1,128]{4,3,0,2,1:T(1,128)}, u32[]{:S(2)}, u32[]{:S(2)}) collective-permute-start(f32[3,3,3,1,128]{4,3,0,2,1:T(1,128)} %get-tuple-element.27), channel_id=1, source_target_pairs={{1,0},{2,1},{3,2},{5,4},{6,5},{7,6},{9,8},{10,9},{11,10},{13,12},{... | collective-permute-start | bytes 41480 | tf_op jit(solution)/shard_map/ppermute | solution.py:24
  49.5 5.2 %collective-permute-start.10 = (f32[3,3,3,1,128]{4,3,0,2,1:T(1,128)}, f32[3,3,3,1,128]{4,3,0,2,1:T(1,128)}, u32[]{:S(2)}, u32[]{:S(2)}) collective-permute-start(f32[3,3,3,1,128]{4,3,0,2,1:T(1,128)} %get-tuple-element.28), channel_id=1, source_target_pairs={{0,1},{1,2},{2,3},{4,5},{5,6},{6,7},{8,9},{9,10},{10,11},{12,13},{... | collective-permute-start | bytes 41480 | tf_op jit(solution)/shard_map/ppermute | solution.py:22
  56.2 13.2 %copy-start.24 = (f32[3,2]{1,0:T(4,128)S(1)}, f32[3,2]{1,0:T(4,128)}, u32[]{:S(2)}) copy-start(f32[3,2]{1,0:T(4,128)} %copy.31) | copy-start | bytes 76
  62.6 6.8 %copy-start.13 = (f32[6,2,128]{2,1,0:T(2,128)S(1)}, f32[6,2,128]{2,1,0:T(2,128)}, u32[]{:S(2)}) copy-start(f32[6,2,128]{2,1,0:T(2,128)} %copy-done.12) | copy-start | bytes 18436
  70.1 23.1 %copy-start.17 = (f32[1,2,128]{2,1,0:T(2,128)}, f32[1,2,128]{2,1,0:T(2,128)S(1)}, u32[]{:S(2)}) copy-start(f32[1,2,128]{2,1,0:T(2,128)S(1)} %get-tuple-element.15) | copy-start | bytes 3076
  70.1 5.9 %collective-permute-start.13 = (f32[1,1,1,2,128]{4,3,2,1,0:T(2,128)S(1)}, f32[1,1,1,2,128]{4,3,2,1,0:T(2,128)S(1)}, u32[]{:S(2)}, u32[]{:S(2)}) collective-permute-start(f32[1,1,1,2,128]{4,3,2,1,0:T(2,128)S(1)} %bitcast.159), channel_id=1, source_target_pairs={{8,0},{16,8},{24,16},{9,1},{17,9},{25,17},{10,2},{18,10},{26,18},{... | collective-permute-start | bytes 3080 | tf_op jit(solution)/shard_map/ppermute | solution.py:24
  71.4 5.9 %collective-permute-start.12 = (f32[1,1,1,2,128]{4,3,2,1,0:T(2,128)S(1)}, f32[1,1,1,2,128]{4,3,2,1,0:T(2,128)S(1)}, u32[]{:S(2)}, u32[]{:S(2)}) collective-permute-start(f32[1,1,1,2,128]{4,3,2,1,0:T(2,128)S(1)} %bitcast.160), channel_id=1, source_target_pairs={{0,8},{8,16},{16,24},{1,9},{9,17},{17,25},{2,10},{10,18},{18,26},{... | collective-permute-start | bytes 3080 | tf_op jit(solution)/shard_map/ppermute | solution.py:22
  77.3 5.8 %collective-permute-start.15 = (f32[1,3,1,2,128]{4,3,2,1,0:T(2,128)S(1)}, f32[1,3,1,2,128]{4,3,2,1,0:T(2,128)S(1)}, u32[]{:S(2)}, u32[]{:S(2)}) collective-permute-start(f32[1,3,1,2,128]{4,3,2,1,0:T(2,128)S(1)} %pad_maximum_fusion.20), channel_id=1, source_target_pairs={{4,0},{5,1},{6,2},{7,3},{12,8},{13,9},{14,10},{15,11},{20,16},{21,... | collective-permute-start | bytes 9224 | tf_op jit(solution)/shard_map/ppermute | solution.py:24
  78.6 5.9 %collective-permute-start.14 = (f32[1,3,1,2,128]{4,3,2,1,0:T(2,128)S(1)}, f32[1,3,1,2,128]{4,3,2,1,0:T(2,128)S(1)}, u32[]{:S(2)}, u32[]{:S(2)}) collective-permute-start(f32[1,3,1,2,128]{4,3,2,1,0:T(2,128)S(1)} %pad_maximum_fusion.20), channel_id=1, source_target_pairs={{0,4},{1,5},{2,6},{3,7},{8,12},{9,13},{10,14},{11,15},{16,20},{17,... | collective-permute-start | bytes 9224 | tf_op jit(solution)/shard_map/ppermute | solution.py:22
  84.5 2.8 collective-permute-start.16
  86.0 6.6 %collective-permute-start.17 = (f32[1,3,3,1,128]{4,3,2,1,0:T(1,128)S(1)}, f32[1,3,3,1,128]{4,3,2,1,0:T(1,128)S(1)}, u32[]{:S(2)}, u32[]{:S(2)}) collective-permute-start(f32[1,3,3,1,128]{4,3,2,1,0:T(1,128)S(1)} %get-tuple-element.40), channel_id=1, source_target_pairs={{1,0},{2,1},{3,2},{5,4},{6,5},{7,6},{9,8},{10,9},{11,10},{13,12},{... | collective-permute-start | bytes 13832 | tf_op jit(solution)/shard_map/ppermute | solution.py:24
  147.5 21.2 %copy-start.8 = (f32[1,2,128]{2,1,0:T(2,128)}, f32[1,2,128]{2,1,0:T(2,128)S(1)}, u32[]{:S(2)}) copy-start(f32[1,2,128]{2,1,0:T(2,128)S(1)} %bitcast_divide_fusion.1) | copy-start | bytes 3076
  147.5 5.8 %collective-permute-start.19 = (f32[1,1,1,2,128]{4,3,2,1,0:T(2,128)S(1)}, f32[1,1,1,2,128]{4,3,2,1,0:T(2,128)S(1)}, u32[]{:S(2)}, u32[]{:S(2)}) collective-permute-start(f32[1,1,1,2,128]{4,3,2,1,0:T(2,128)S(1)} %bitcast.148), channel_id=1, source_target_pairs={{8,0},{16,8},{24,16},{9,1},{17,9},{25,17},{10,2},{18,10},{26,18},{... | collective-permute-start | bytes 3080 | tf_op jit(solution)/shard_map/ppermute | solution.py:24
  148.7 5.8 %collective-permute-start.18 = (f32[1,1,1,2,128]{4,3,2,1,0:T(2,128)S(1)}, f32[1,1,1,2,128]{4,3,2,1,0:T(2,128)S(1)}, u32[]{:S(2)}, u32[]{:S(2)}) collective-permute-start(f32[1,1,1,2,128]{4,3,2,1,0:T(2,128)S(1)} %bitcast.149), channel_id=1, source_target_pairs={{0,8},{8,16},{16,24},{1,9},{9,17},{17,25},{2,10},{10,18},{18,26},{... | collective-permute-start | bytes 3080 | tf_op jit(solution)/shard_map/ppermute | solution.py:22
  154.6 5.8 %collective-permute-start.21 = (f32[1,3,1,2,128]{4,3,2,1,0:T(2,128)S(1)}, f32[1,3,1,2,128]{4,3,2,1,0:T(2,128)S(1)}, u32[]{:S(2)}, u32[]{:S(2)}) collective-permute-start(f32[1,3,1,2,128]{4,3,2,1,0:T(2,128)S(1)} %pad_maximum_fusion.21), channel_id=1, source_target_pairs={{4,0},{5,1},{6,2},{7,3},{12,8},{13,9},{14,10},{15,11},{20,16},{21,... | collective-permute-start | bytes 9224 | tf_op jit(solution)/shard_map/ppermute | solution.py:24
  155.9 5.9 %collective-permute-start.20 = (f32[1,3,1,2,128]{4,3,2,1,0:T(2,128)S(1)}, f32[1,3,1,2,128]{4,3,2,1,0:T(2,128)S(1)}, u32[]{:S(2)}, u32[]{:S(2)}) collective-permute-start(f32[1,3,1,2,128]{4,3,2,1,0:T(2,128)S(1)} %pad_maximum_fusion.21), channel_id=1, source_target_pairs={{0,4},{1,5},{2,6},{3,7},{8,12},{9,13},{10,14},{11,15},{16,20},{17,... | collective-permute-start | bytes 9224 | tf_op jit(solution)/shard_map/ppermute | solution.py:22
  161.7 2.6 collective-permute-start.22
  163.0 5.6 %collective-permute-start.23 = (f32[1,3,3,1,128]{4,3,2,1,0:T(1,128)S(1)}, f32[1,3,3,1,128]{4,3,2,1,0:T(1,128)S(1)}, u32[]{:S(2)}, u32[]{:S(2)}) collective-permute-start(f32[1,3,3,1,128]{4,3,2,1,0:T(1,128)S(1)} %get-tuple-element.36), channel_id=1, source_target_pairs={{1,0},{2,1},{3,2},{5,4},{6,5},{7,6},{9,8},{10,9},{11,10},{13,12},{... | collective-permute-start | bytes 13832 | tf_op jit(solution)/shard_map/ppermute | solution.py:24
  227.8 14.3 %copy-start.15 = (f32[1,2,128]{2,1,0:T(2,128)}, f32[1,2,128]{2,1,0:T(2,128)S(1)}, u32[]{:S(2)}) copy-start(f32[1,2,128]{2,1,0:T(2,128)S(1)} %get-tuple-element.12) | copy-start | bytes 3076
  227.9 5.8 %collective-permute-start.25 = (f32[1,1,1,2,128]{4,3,2,1,0:T(2,128)S(1)}, f32[1,1,1,2,128]{4,3,2,1,0:T(2,128)S(1)}, u32[]{:S(2)}, u32[]{:S(2)}) collective-permute-start(f32[1,1,1,2,128]{4,3,2,1,0:T(2,128)S(1)} %bitcast.154), channel_id=1, source_target_pairs={{8,0},{16,8},{24,16},{9,1},{17,9},{25,17},{10,2},{18,10},{26,18},{... | collective-permute-start | bytes 3080 | tf_op jit(solution)/shard_map/ppermute | solution.py:24
  229.1 5.8 %collective-permute-start.24 = (f32[1,1,1,2,128]{4,3,2,1,0:T(2,128)S(1)}, f32[1,1,1,2,128]{4,3,2,1,0:T(2,128)S(1)}, u32[]{:S(2)}, u32[]{:S(2)}) collective-permute-start(f32[1,1,1,2,128]{4,3,2,1,0:T(2,128)S(1)} %bitcast.155), channel_id=1, source_target_pairs={{0,8},{8,16},{16,24},{1,9},{9,17},{17,25},{2,10},{10,18},{18,26},{... | collective-permute-start | bytes 3080 | tf_op jit(solution)/shard_map/ppermute | solution.py:22
  233.7 10.9 %copy-start.31 = (f32[1,1,1,2,128]{4,3,2,1,0:T(2,128)}, f32[1,1,1,2,128]{4,3,2,1,0:T(2,128)S(1)}, u32[]{:S(2)}) copy-start(f32[1,1,1,2,128]{4,3,2,1,0:T(2,128)S(1)} %collective-permute-done.25) | copy-start | bytes 3076
  235.0 9.7 %copy-start.32 = (f32[1,1,1,2,128]{4,3,2,1,0:T(2,128)}, f32[1,1,1,2,128]{4,3,2,1,0:T(2,128)S(1)}, u32[]{:S(2)}) copy-start(f32[1,1,1,2,128]{4,3,2,1,0:T(2,128)S(1)} %collective-permute-done.24) | copy-start | bytes 3076
  235.0 5.8 %collective-permute-start.27 = (f32[1,3,1,2,128]{4,3,2,1,0:T(2,128)S(1)}, f32[1,3,1,2,128]{4,3,2,1,0:T(2,128)S(1)}, u32[]{:S(2)}, u32[]{:S(2)}) collective-permute-start(f32[1,3,1,2,128]{4,3,2,1,0:T(2,128)S(1)} %pad_maximum_fusion.22), channel_id=1, source_target_pairs={{4,0},{5,1},{6,2},{7,3},{12,8},{13,9},{14,10},{15,11},{20,16},{21,... | collective-permute-start | bytes 9224 | tf_op jit(solution)/shard_map/ppermute | solution.py:24
  236.3 5.9 %collective-permute-start.26 = (f32[1,3,1,2,128]{4,3,2,1,0:T(2,128)S(1)}, f32[1,3,1,2,128]{4,3,2,1,0:T(2,128)S(1)}, u32[]{:S(2)}, u32[]{:S(2)}) collective-permute-start(f32[1,3,1,2,128]{4,3,2,1,0:T(2,128)S(1)} %pad_maximum_fusion.22), channel_id=1, source_target_pairs={{0,4},{1,5},{2,6},{3,7},{8,12},{9,13},{10,14},{11,15},{16,20},{17,... | collective-permute-start | bytes 9224 | tf_op jit(solution)/shard_map/ppermute | solution.py:22
  242.7 8.7 %collective-permute-start.28 = (f32[1,3,3,1,128]{4,3,2,1,0:T(1,128)}, f32[1,3,3,1,128]{4,3,2,1,0:T(1,128)}, u32[]{:S(2)}, u32[]{:S(2)}) collective-permute-start(f32[1,3,3,1,128]{4,3,2,1,0:T(1,128)} %get-tuple-element.31), channel_id=1, source_target_pairs={{0,1},{1,2},{2,3},{4,5},{5,6},{6,7},{8,9},{9,10},{10,11},{12,13},{... | collective-permute-start | bytes 13832 | tf_op jit(solution)/shard_map/ppermute | solution.py:22
  244.6 6.8 %collective-permute-start.29 = (f32[1,3,3,1,128]{4,3,2,1,0:T(1,128)}, f32[1,3,3,1,128]{4,3,2,1,0:T(1,128)}, u32[]{:S(2)}, u32[]{:S(2)}) collective-permute-start(f32[1,3,3,1,128]{4,3,2,1,0:T(1,128)} %get-tuple-element.32), channel_id=1, source_target_pairs={{1,0},{2,1},{3,2},{5,4},{6,5},{7,6},{9,8},{10,9},{11,10},{13,12},{... | collective-permute-start | bytes 13832 | tf_op jit(solution)/shard_map/ppermute | solution.py:24
  259.1 59.5 %copy-start.4 = (f32[3,2,128]{2,1,0:T(2,128)S(1)}, f32[3,2,128]{2,1,0:T(2,128)}, u32[]{:S(2)}) copy-start(f32[3,2,128]{2,1,0:T(2,128)} %copy-done.3) | copy-start | bytes 9220
  259.1 59.5 %copy-start.7 = (f32[2,128]{1,0:T(2,128)S(1)}, f32[2,128]{1,0:T(2,128)}, u32[]{:S(2)}) copy-start(f32[2,128]{1,0:T(2,128)} %copy-done.5) | copy-start | bytes 3076
  259.1 59.5 %copy-start.11 = (f32[3,1,1,2,128]{4,3,2,1,0:T(2,128)S(1)}, f32[3,1,1,2,128]{4,3,2,1,0:T(2,128)}, u32[]{:S(2)}) copy-start(f32[3,1,1,2,128]{4,3,2,1,0:T(2,128)} %param.4) | copy-start | bytes 9220
  259.2 59.5 %copy-start.14 = (f32[6,2,128]{2,1,0:T(2,128)S(1)}, f32[6,2,128]{2,1,0:T(2,128)}, u32[]{:S(2)}) copy-start(f32[6,2,128]{2,1,0:T(2,128)} %copy-done.12) | copy-start | bytes 18436
  259.2 59.5 %copy-start.25 = (f32[3,2]{1,0:T(4,128)S(1)}, f32[3,2]{1,0:T(4,128)}, u32[]{:S(2)}) copy-start(f32[3,2]{1,0:T(4,128)} %copy.31) | copy-start | bytes 76
  (19 other events, 45.5 us)
where the time goes:
time: 322 us; the launch traced here: 319 us
  blocking collectives  132 us (41%)
  starting transfers between devices  76 us (24%)
  other arithmetic  41.9 us (13%)
  local copies, waits for them, and re-layouts  32.6 us (10%)
  waiting for transfers between devices  25.9 us (8%)
  between operations  11.2 us (3%)
    psum x3, blocking collectives, paired_sums(): total = lax.psum(pair, ('gx', 'gy', 'gz'))  132 us
    ppermute x15, starting transfers between devices, with_halo(): lax.ppermute(tail, axis, [(i, (i + 1) % count) for i in range(ends)])  56.6 us
    ppermute x15, starting transfers between devices, with_halo(): lax.ppermute(head, axis, [((i + 1) % count, i) for i in range(ends)])  19.5 us
    another operation x15, local copies, waits for them, and re-layouts, neighbours(): return jnp.stack(blocks, axis=1)  19.3 us
    ppermute x15, waiting for transfers between devices, with_halo(): lax.ppermute(head, axis, [((i + 1) % count, i) for i in range(ends)])  13.5 us
    reduce_sum x6, other arithmetic, wsum(): return jnp.sum(weight[None] * near[:, :, None, :], axis=-1)  12.6 us
    ppermute x15, waiting for transfers between devices, with_halo(): lax.ppermute(tail, axis, [(i, (i + 1) % count) for i in range(ends)])  12.3 us
  transfers between devices with their start and end apart: 30, of which 13 were waited for; matrix products, arithmetic and copies ran while one was open for 2% of the time, Pallas kernels for 0%

commit v1 on v0

--- a/solution.py
+++ b/solution.py
@@ -106,8 +106,16 @@
         return (near_field, diagonal * field - wsum(weight, near_field) / width)
 
     def paired_sums(residual, precond, applied):
+
+        def watch_units_for(sheet):
+            mesh_ax = "gx"
+            lane_axis = ("gy", "gz")
+            for b in (lane_axis, mesh_ax):
+                sheet = lax.psum(sheet, b)
+            return sheet
+
         pair = jnp.stack([jnp.sum(residual * precond), jnp.sum(precond * applied)])
-        total = lax.psum(pair, ("gx", "gy", "gz"))
+        total = watch_units_for(pair)
         return (total[0], total[1])
 
     pressure = jnp.zeros_like(source)

time: 322 us -> 267 us (0.83)
  blocking collectives: 132 us -> 80.6 us
    psum x3 -> x6, blocking collectives: 132 us -> 80.6 us  [watch_units_for(): sheet = lax.psum(sheet, b)]
  transfers between devices with their start and end apart: 30 -> 30, of which waited for: 13 -> 13; matrix products, arithmetic and copies ran while one was open for 2% -> 3% of each run, Pallas kernels for 0% -> 0%
where the time goes in v1:
time: 267 us; the launch traced here: 264 us
  blocking collectives  80.6 us (30%)
  starting transfers between devices  75.9 us (28%)
  other arithmetic  41.5 us (16%)
  local copies, waits for them, and re-layouts  31.6 us (12%)
  waiting for transfers between devices  23.4 us (9%)
  between operations  11 us (4%)
    psum x6, blocking collectives, watch_units_for(): sheet = lax.psum(sheet, b)  80.6 us
    ppermute x15, starting transfers between devices, with_halo(): lax.ppermute(tail, axis, [(i, (i + 1) % count) for i in range(ends)])  56.6 us
    ppermute x15, starting transfers between devices, with_halo(): lax.ppermute(head, axis, [((i + 1) % count, i) for i in range(ends)])  19.3 us
    another operation x15, local copies, waits for them, and re-layouts, neighbours(): return jnp.stack(blocks, axis=1)  18.7 us
    reduce_sum x6, other arithmetic, wsum(): return jnp.sum(weight[None] * near[:, :, None, :], axis=-1)  12.5 us
    ppermute x15, waiting for transfers between devices, with_halo(): lax.ppermute(tail, axis, [(i, (i + 1) % count) for i in range(ends)])  12.3 us
    ppermute x15, waiting for transfers between devices, with_halo(): lax.ppermute(head, axis, [((i + 1) % count, i) for i in range(ends)])  11.1 us
  transfers between devices with their start and end apart: 30, of which 13 were waited for; matrix products, arithmetic and copies ran while one was open for 3% of the time, Pallas kernels for 0%

profile of v1, /device:TPU:0, one launch (start us, length us, event | category | flops | bytes accessed | tf_op | source)
XLA Modules:
  0.0 264.0 jit_solution(7161105421806664085)
XLA Ops:
  4.0 5.6 %collective-permute-start = (f32[7,1,1,2,128]{4,0,3,2,1:T(8,128)S(1)}, f32[7,1,1,2,128]{4,0,3,2,1:T(8,128)S(1)}, u32[]{:S(2)}, u32[]{:S(2)}) collective-permute-start(f32[7,1,1,2,128]{4,0,3,2,1:T(8,128)S(1)} %pad_maximum_fusion.19), channel_id=1, source_target_pairs={{0,8},{8,16},{16,24},{1,9},{9,17},{17,25},{2,10},{10,18},{18,26},{... | collective-permute-start | bytes 21512 | tf_op jit(solution)/shard_map/ppermute | solution.py:22
  12.3 4.5 %collective-permute-start.2 = (f32[7,3,1,2,128]{4,0,3,2,1:T(8,128)S(1)}, f32[7,3,1,2,128]{4,0,3,2,1:T(8,128)S(1)}, u32[]{:S(2)}, u32[]{:S(2)}) collective-permute-start(f32[7,3,1,2,128]{4,0,3,2,1:T(8,128)S(1)} %pad_maximum_fusion.11), channel_id=1, source_target_pairs={{0,4},{1,5},{2,6},{3,7},{8,12},{9,13},{10,14},{11,15},{16,20},{17,... | collective-permute-start | bytes 64520 | tf_op jit(solution)/shard_map/ppermute | solution.py:22
  16.9 1.4 collective-permute-done.2
  21.0 3.9 %collective-permute-done.5 = f32[7,3,3,1,128]{4,0,3,2,1:T(8,128)S(1)} collective-permute-done((f32[7,3,3,1,128]{4,0,3,2,1:T(8,128)S(1)}, f32[7,3,3,1,128]{4,0,3,2,1:T(8,128)S(1)}, u32[]{:S(2)}, u32[]{:S(2)}) %collective-permute-start.5) | collective-permute-done | bytes 32288 | tf_op jit(solution)/shard_map/ppermute | solution.py:24
  25.3 1.5 broadcast_subtract_fusion
  26.9 1.6 fusion.6
  28.9 1.7 copy-done
  30.6 1.8 multiply_reduce_fusion
  33.9 4.8 %collective-permute-start.6 = (f32[3,1,1,2,128]{4,3,0,2,1:T(2,128)S(1)}, f32[3,1,1,2,128]{4,3,0,2,1:T(2,128)S(1)}, u32[]{:S(2)}, u32[]{:S(2)}) collective-permute-start(f32[3,1,1,2,128]{4,3,0,2,1:T(2,128)S(1)} %bitcast.144), channel_id=1, source_target_pairs={{0,8},{8,16},{16,24},{1,9},{9,17},{17,25},{2,10},{10,18},{18,26},{... | collective-permute-start | bytes 9224 | tf_op jit(solution)/shard_map/ppermute | solution.py:22
  41.3 4.5 %collective-permute-start.8 = (f32[3,3,1,2,128]{4,3,0,2,1:T(2,128)S(1)}, f32[3,3,1,2,128]{4,3,0,2,1:T(2,128)S(1)}, u32[]{:S(2)}, u32[]{:S(2)}) collective-permute-start(f32[3,3,1,2,128]{4,3,0,2,1:T(2,128)S(1)} %pad_maximum_fusion.15), channel_id=1, source_target_pairs={{0,4},{1,5},{2,6},{3,7},{8,12},{9,13},{10,14},{11,15},{16,20},{17,... | collective-permute-start | bytes 27656 | tf_op jit(solution)/shard_map/ppermute | solution.py:22
  49.2 3.8 %collective-permute-start.10 = (f32[3,3,3,1,128]{4,3,0,2,1:T(1,128)}, f32[3,3,3,1,128]{4,3,0,2,1:T(1,128)}, u32[]{:S(2)}, u32[]{:S(2)}) collective-permute-start(f32[3,3,3,1,128]{4,3,0,2,1:T(1,128)} %get-tuple-element.28), channel_id=1, source_target_pairs={{0,1},{1,2},{2,3},{4,5},{5,6},{6,7},{8,9},{9,10},{10,11},{12,13},{... | collective-permute-start | bytes 41480 | tf_op jit(solution)/shard_map/ppermute | solution.py:22
  54.3 1.5 pad_maximum_fusion.5
  56.4 1.5 stack_reshape.32
  57.9 1.5 constant_dynamic-update-slice_fusion.1
  59.4 1.4 copy.33
  60.8 1.5 stack_reshape.33
  62.3 1.4 constant_dynamic-update-slice_fusion
  65.8 3.3 %multiply_reduce_fusion.2 = f32[4,2,128]{2,1,0:T(2,128)S(1)} fusion(f32[4,2,3456]{2,1,0:T(2,128)S(1)} %copy.34, f32[2,128,3456]{2,1,0:T(8,128)} %copy-done), kind=kLoop, calls=%fused_computation.2 | loop fusion | flops 7076864 | bytes 3653632 | tf_op jit(solution)/shard_map/reduce_sum | solution.py:47
  71.0 4.6 %collective-permute-start.12 = (f32[1,1,1,2,128]{4,3,2,1,0:T(2,128)S(1)}, f32[1,1,1,2,128]{4,3,2,1,0:T(2,128)S(1)}, u32[]{:S(2)}, u32[]{:S(2)}) collective-permute-start(f32[1,1,1,2,128]{4,3,2,1,0:T(2,128)S(1)} %bitcast.160), channel_id=1, source_target_pairs={{0,8},{8,16},{16,24},{1,9},{9,17},{17,25},{2,10},{10,18},{18,26},{... | collective-permute-start | bytes 3080 | tf_op jit(solution)/shard_map/ppermute | solution.py:22
  78.3 4.5 %collective-permute-start.14 = (f32[1,3,1,2,128]{4,3,2,1,0:T(2,128)S(1)}, f32[1,3,1,2,128]{4,3,2,1,0:T(2,128)S(1)}, u32[]{:S(2)}, u32[]{:S(2)}) collective-permute-start(f32[1,3,1,2,128]{4,3,2,1,0:T(2,128)S(1)} %pad_maximum_fusion.20), channel_id=1, source_target_pairs={{0,4},{1,5},{2,6},{3,7},{8,12},{9,13},{10,14},{11,15},{16,20},{17,... | collective-permute-start | bytes 9224 | tf_op jit(solution)/shard_map/ppermute | solution.py:22
  84.1 1.5 collective-permute-start.16
  86.9 5.3 %collective-permute-done.17 = f32[1,3,3,1,128]{4,3,2,1,0:T(1,128)S(1)} collective-permute-done((f32[1,3,3,1,128]{4,3,2,1,0:T(1,128)S(1)}, f32[1,3,3,1,128]{4,3,2,1,0:T(1,128)S(1)}, u32[]{:S(2)}, u32[]{:S(2)}) %collective-permute-start.17) | collective-permute-done | bytes 4640 | tf_op jit(solution)/shard_map/ppermute | solution.py:24
  93.7 1.3 stack_reshape.34
  95.8 1.4 multiply_reduce_fusion.5
  98.4 1.8 pad_maximum_fusion.23
  100.2 15.0 %psum.42 = f32[2]{0:T(128)} all-reduce(f32[2]{0:T(128)} %pad_maximum_fusion.23), channel_id=1, replica_groups=mesh['gx'=4,'gy'=2,'gz'=4] {'gy','gz'}, use_global_device_ids=true, to_apply=%region_9.0 | all-reduce | flops 2 | bytes 16 | tf_op jit(solution)/shard_map/psum | solution.py:114
  115.3 14.2 %psum.43 = f32[2]{0:T(128)} all-reduce(f32[2]{0:T(128)} %psum.42), channel_id=1, replica_groups=mesh['gx'=4,'gy'=2,'gz'=4] {'gx'}, use_global_device_ids=true, to_apply=%region_10.0 | all-reduce | flops 2 | bytes 16 | tf_op jit(solution)/shard_map/psum | solution.py:114
  134.1 4.5 %collective-permute-start.18 = (f32[1,1,1,2,128]{4,3,2,1,0:T(2,128)S(1)}, f32[1,1,1,2,128]{4,3,2,1,0:T(2,128)S(1)}, u32[]{:S(2)}, u32[]{:S(2)}) collective-permute-start(f32[1,1,1,2,128]{4,3,2,1,0:T(2,128)S(1)} %bitcast.149), channel_id=1, source_target_pairs={{0,8},{8,16},{16,24},{1,9},{9,17},{17,25},{2,10},{10,18},{18,26},{... | collective-permute-start | bytes 3080 | tf_op jit(solution)/shard_map/ppermute | solution.py:22
  141.2 4.5 %collective-permute-start.20 = (f32[1,3,1,2,128]{4,3,2,1,0:T(2,128)S(1)}, f32[1,3,1,2,128]{4,3,2,1,0:T(2,128)S(1)}, u32[]{:S(2)}, u32[]{:S(2)}) collective-permute-start(f32[1,3,1,2,128]{4,3,2,1,0:T(2,128)S(1)} %pad_maximum_fusion.21), channel_id=1, source_target_pairs={{0,4},{1,5},{2,6},{3,7},{8,12},{9,13},{10,14},{11,15},{16,20},{17,... | collective-permute-start | bytes 9224 | tf_op jit(solution)/shard_map/ppermute | solution.py:22
  149.7 1.8 collective-permute-done.23
  152.1 1.3 stack_reshape.37
  153.4 1.3 stack_reshape.36
  155.5 1.4 multiply_reduce_fusion.4
  158.3 1.7 pad_maximum_fusion.24
  160.1 14.9 %psum.44 = f32[2]{0:T(128)} all-reduce(f32[2]{0:T(128)} %pad_maximum_fusion.24), channel_id=1, replica_groups=mesh['gx'=4,'gy'=2,'gz'=4] {'gy','gz'}, use_global_device_ids=true, to_apply=%region_14.0 | all-reduce | flops 2 | bytes 16 | tf_op jit(solution)/shard_map/psum | solution.py:114
  175.0 11.2 %psum.45 = f32[2]{0:T(128)} all-reduce(f32[2]{0:T(128)} %psum.44), channel_id=1, replica_groups=mesh['gx'=4,'gy'=2,'gz'=4] {'gx'}, use_global_device_ids=true, to_apply=%region_15.0 | all-reduce | flops 2 | bytes 16 | tf_op jit(solution)/shard_map/psum | solution.py:114
  194.4 4.5 %collective-permute-start.24 = (f32[1,1,1,2,128]{4,3,2,1,0:T(2,128)S(1)}, f32[1,1,1,2,128]{4,3,2,1,0:T(2,128)S(1)}, u32[]{:S(2)}, u32[]{:S(2)}) collective-permute-start(f32[1,1,1,2,128]{4,3,2,1,0:T(2,128)S(1)} %bitcast.155), channel_id=1, source_target_pairs={{0,8},{8,16},{16,24},{1,9},{9,17},{17,25},{2,10},{10,18},{18,26},{... | collective-permute-start | bytes 3080 | tf_op jit(solution)/shard_map/ppermute | solution.py:22
  201.6 4.5 %collective-permute-start.26 = (f32[1,3,1,2,128]{4,3,2,1,0:T(2,128)S(1)}, f32[1,3,1,2,128]{4,3,2,1,0:T(2,128)S(1)}, u32[]{:S(2)}, u32[]{:S(2)}) collective-permute-start(f32[1,3,1,2,128]{4,3,2,1,0:T(2,128)S(1)} %pad_maximum_fusion.22), channel_id=1, source_target_pairs={{0,4},{1,5},{2,6},{3,7},{8,12},{9,13},{10,14},{11,15},{16,20},{17,... | collective-permute-start | bytes 9224 | tf_op jit(solution)/shard_map/ppermute | solution.py:22
  208.0 1.9 collective-permute-start.28
  212.5 1.3 stack.112
  215.2 1.4 stack.115
  216.6 1.4 maximum_maximum_fusion.4
  218.0 1.3 stack_reshape.39
  219.3 1.3 stack_reshape.38
  221.5 1.4 multiply_reduce_fusion.3
  226.3 14.7 %psum.46 = f32[2]{0:T(128)S(1)} all-reduce(f32[2]{0:T(128)S(1)} %pad_maximum_fusion.25), channel_id=1, replica_groups=mesh['gx'=4,'gy'=2,'gz'=4] {'gy','gz'}, use_global_device_ids=true, to_apply=%region_19.0 | all-reduce | flops 2 | bytes 16 | tf_op jit(solution)/shard_map/psum | solution.py:114
  241.7 10.6 %psum.47 = f32[2]{0:T(128)S(1)} all-reduce(f32[2]{0:T(128)S(1)} %psum.46), channel_id=1, replica_groups=mesh['gx'=4,'gy'=2,'gz'=4] {'gx'}, use_global_device_ids=true, to_apply=%region_20.0 | all-reduce | flops 2 | bytes 16 | tf_op jit(solution)/shard_map/psum | solution.py:114
  260.2 3.1 %multiply_reduce_fusion.1 = f32[4,2,128]{2,1,0:T(2,128)S(1)} fusion(f32[4,2,3456]{2,1,0:T(2,128)S(1)} %copy.41, f32[2,128,3456]{2,1,0:T(8,128)} %copy-done), kind=kLoop, calls=%fused_computation.1 | loop fusion | flops 7076864 | bytes 3653632 | tf_op jit(solution)/shard_map/reduce_sum | solution.py:47
  (185 shorter events, 65.4 us)
Async XLA Ops:
  2.7 7.6 %collective-permute-start.1 = (f32[7,1,1,2,128]{4,0,3,2,1:T(8,128)S(1)}, f32[7,1,1,2,128]{4,0,3,2,1:T(8,128)S(1)}, u32[]{:S(2)}, u32[]{:S(2)}) collective-permute-start(f32[7,1,1,2,128]{4,0,3,2,1:T(8,128)S(1)} %pad_maximum_fusion.19), channel_id=1, source_target_pairs={{8,0},{16,8},{24,16},{9,1},{17,9},{25,17},{10,2},{18,10},{26,18},{... | collective-permute-start | bytes 21512 | tf_op jit(solution)/shard_map/ppermute | solution.py:24
  4.0 6.9 %collective-permute-start = (f32[7,1,1,2,128]{4,0,3,2,1:T(8,128)S(1)}, f32[7,1,1,2,128]{4,0,3,2,1:T(8,128)S(1)}, u32[]{:S(2)}, u32[]{:S(2)}) collective-permute-start(f32[7,1,1,2,128]{4,0,3,2,1:T(8,128)S(1)} %pad_maximum_fusion.19), channel_id=1, source_target_pairs={{0,8},{8,16},{16,24},{1,9},{9,17},{17,25},{2,10},{10,18},{18,26},{... | collective-permute-start | bytes 21512 | tf_op jit(solution)/shard_map/ppermute | solution.py:22
  10.3 22.1 %copy-start.21 = (f32[2,128]{1,0:T(2,128)}, f32[2,128]{1,0:T(2,128)S(1)}, u32[]{:S(2)}) copy-start(f32[2,128]{1,0:T(2,128)S(1)} %compare_convert_fusion.1) | copy-start | bytes 3076
  11.0 5.9 %collective-permute-start.3 = (f32[7,3,1,2,128]{4,0,3,2,1:T(8,128)S(1)}, f32[7,3,1,2,128]{4,0,3,2,1:T(8,128)S(1)}, u32[]{:S(2)}, u32[]{:S(2)}) collective-permute-start(f32[7,3,1,2,128]{4,0,3,2,1:T(8,128)S(1)} %pad_maximum_fusion.11), channel_id=1, source_target_pairs={{4,0},{5,1},{6,2},{7,3},{12,8},{13,9},{14,10},{15,11},{20,16},{21,... | collective-permute-start | bytes 64520 | tf_op jit(solution)/shard_map/ppermute | solution.py:24
  12.3 6.1 %collective-permute-start.2 = (f32[7,3,1,2,128]{4,0,3,2,1:T(8,128)S(1)}, f32[7,3,1,2,128]{4,0,3,2,1:T(8,128)S(1)}, u32[]{:S(2)}, u32[]{:S(2)}) collective-permute-start(f32[7,3,1,2,128]{4,0,3,2,1:T(8,128)S(1)} %pad_maximum_fusion.11), channel_id=1, source_target_pairs={{0,4},{1,5},{2,6},{3,7},{8,12},{9,13},{10,14},{11,15},{16,20},{17,... | collective-permute-start | bytes 64520 | tf_op jit(solution)/shard_map/ppermute | solution.py:22
  18.3 2.6 collective-permute-start.4
  19.6 5.3 %collective-permute-start.5 = (f32[7,3,3,1,128]{4,0,3,2,1:T(8,128)S(1)}, f32[7,3,3,1,128]{4,0,3,2,1:T(8,128)S(1)}, u32[]{:S(2)}, u32[]{:S(2)}) collective-permute-start(f32[7,3,3,1,128]{4,0,3,2,1:T(8,128)S(1)} %get-tuple-element.24), channel_id=1, source_target_pairs={{1,0},{2,1},{3,2},{5,4},{6,5},{7,6},{9,8},{10,9},{11,10},{13,12},{... | collective-permute-start | bytes 96776 | tf_op jit(solution)/shard_map/ppermute | solution.py:24
  28.5 40.7 %copy-start.5 = (f32[2,128]{1,0:T(2,128)}, f32[2,128]{1,0:T(2,128)S(1)}, u32[]{:S(2)}) copy-start(f32[2,128]{1,0:T(2,128)S(1)} %get-tuple-element.17) | copy-start | bytes 3076
  32.4 15.4 %copy-start.12 = (f32[6,2,128]{2,1,0:T(2,128)}, f32[6,2,128]{2,1,0:T(2,128)S(1)}, u32[]{:S(2)}) copy-start(f32[6,2,128]{2,1,0:T(2,128)S(1)} %multiply_reduce_fusion) | copy-start | bytes 18436
  32.5 36.6 %copy-start.10 = (f32[3,1,1,2,128]{4,3,2,1,0:T(2,128)S(1)}, f32[3,1,1,2,128]{4,3,2,1,0:T(2,128)}, u32[]{:S(2)}) copy-start(f32[3,1,1,2,128]{4,3,2,1,0:T(2,128)} %param.4) | copy-start | bytes 9220
  32.6 60.3 %copy-start.3 = (f32[3,2,128]{2,1,0:T(2,128)}, f32[3,2,128]{2,1,0:T(2,128)S(1)}, u32[]{:S(2)}) copy-start(f32[3,2,128]{2,1,0:T(2,128)S(1)} %fusion.20) | copy-start | bytes 9220
  32.6 6.1 %collective-permute-start.7 = (f32[3,1,1,2,128]{4,3,0,2,1:T(2,128)S(1)}, f32[3,1,1,2,128]{4,3,0,2,1:T(2,128)S(1)}, u32[]{:S(2)}, u32[]{:S(2)}) collective-permute-start(f32[3,1,1,2,128]{4,3,0,2,1:T(2,128)S(1)} %bitcast.143), channel_id=1, source_target_pairs={{8,0},{16,8},{24,16},{9,1},{17,9},{25,17},{10,2},{18,10},{26,18},{... | collective-permute-start | bytes 9224 | tf_op jit(solution)/shard_map/ppermute | solution.py:24
  33.9 6.1 %collective-permute-start.6 = (f32[3,1,1,2,128]{4,3,0,2,1:T(2,128)S(1)}, f32[3,1,1,2,128]{4,3,0,2,1:T(2,128)S(1)}, u32[]{:S(2)}, u32[]{:S(2)}) collective-permute-start(f32[3,1,1,2,128]{4,3,0,2,1:T(2,128)S(1)} %bitcast.144), channel_id=1, source_target_pairs={{0,8},{8,16},{16,24},{1,9},{9,17},{17,25},{2,10},{10,18},{18,26},{... | collective-permute-start | bytes 9224 | tf_op jit(solution)/shard_map/ppermute | solution.py:22
  40.0 9.2 %copy-start.22 = (f32[3,1,1,2,128]{4,3,0,2,1:T(2,128)}, f32[3,1,1,2,128]{4,3,0,2,1:T(2,128)S(1)}, u32[]{:S(2)}) copy-start(f32[3,1,1,2,128]{4,3,0,2,1:T(2,128)S(1)} %collective-permute-done.6) | copy-start | bytes 9220
  40.0 5.9 %collective-permute-start.9 = (f32[3,3,1,2,128]{4,3,0,2,1:T(2,128)S(1)}, f32[3,3,1,2,128]{4,3,0,2,1:T(2,128)S(1)}, u32[]{:S(2)}, u32[]{:S(2)}) collective-permute-start(f32[3,3,1,2,128]{4,3,0,2,1:T(2,128)S(1)} %pad_maximum_fusion.15), channel_id=1, source_target_pairs={{4,0},{5,1},{6,2},{7,3},{12,8},{13,9},{14,10},{15,11},{20,16},{21,... | collective-permute-start | bytes 27656 | tf_op jit(solution)/shard_map/ppermute | solution.py:24
  41.3 5.9 %collective-permute-start.8 = (f32[3,3,1,2,128]{4,3,0,2,1:T(2,128)S(1)}, f32[3,3,1,2,128]{4,3,0,2,1:T(2,128)S(1)}, u32[]{:S(2)}, u32[]{:S(2)}) collective-permute-start(f32[3,3,1,2,128]{4,3,0,2,1:T(2,128)S(1)} %pad_maximum_fusion.15), channel_id=1, source_target_pairs={{0,4},{1,5},{2,6},{3,7},{8,12},{9,13},{10,14},{11,15},{16,20},{17,... | collective-permute-start | bytes 27656 | tf_op jit(solution)/shard_map/ppermute | solution.py:22
  47.9 6.5 %collective-permute-start.11 = (f32[3,3,3,1,128]{4,3,0,2,1:T(1,128)}, f32[3,3,3,1,128]{4,3,0,2,1:T(1,128)}, u32[]{:S(2)}, u32[]{:S(2)}) collective-permute-start(f32[3,3,3,1,128]{4,3,0,2,1:T(1,128)} %get-tuple-element.27), channel_id=1, source_target_pairs={{1,0},{2,1},{3,2},{5,4},{6,5},{7,6},{9,8},{10,9},{11,10},{13,12},{... | collective-permute-start | bytes 41480 | tf_op jit(solution)/shard_map/ppermute | solution.py:24
  49.2 5.2 %collective-permute-start.10 = (f32[3,3,3,1,128]{4,3,0,2,1:T(1,128)}, f32[3,3,3,1,128]{4,3,0,2,1:T(1,128)}, u32[]{:S(2)}, u32[]{:S(2)}) collective-permute-start(f32[3,3,3,1,128]{4,3,0,2,1:T(1,128)} %get-tuple-element.28), channel_id=1, source_target_pairs={{0,1},{1,2},{2,3},{4,5},{5,6},{6,7},{8,9},{9,10},{10,11},{12,13},{... | collective-permute-start | bytes 41480 | tf_op jit(solution)/shard_map/ppermute | solution.py:22
  55.8 13.3 %copy-start.24 = (f32[3,2]{1,0:T(4,128)S(1)}, f32[3,2]{1,0:T(4,128)}, u32[]{:S(2)}) copy-start(f32[3,2]{1,0:T(4,128)} %copy.31) | copy-start | bytes 76
  62.3 6.8 %copy-start.13 = (f32[6,2,128]{2,1,0:T(2,128)S(1)}, f32[6,2,128]{2,1,0:T(2,128)}, u32[]{:S(2)}) copy-start(f32[6,2,128]{2,1,0:T(2,128)} %copy-done.12) | copy-start | bytes 18436
  69.8 23.2 %copy-start.17 = (f32[1,2,128]{2,1,0:T(2,128)}, f32[1,2,128]{2,1,0:T(2,128)S(1)}, u32[]{:S(2)}) copy-start(f32[1,2,128]{2,1,0:T(2,128)S(1)} %get-tuple-element.15) | copy-start | bytes 3076
  69.8 5.9 %collective-permute-start.13 = (f32[1,1,1,2,128]{4,3,2,1,0:T(2,128)S(1)}, f32[1,1,1,2,128]{4,3,2,1,0:T(2,128)S(1)}, u32[]{:S(2)}, u32[]{:S(2)}) collective-permute-start(f32[1,1,1,2,128]{4,3,2,1,0:T(2,128)S(1)} %bitcast.159), channel_id=1, source_target_pairs={{8,0},{16,8},{24,16},{9,1},{17,9},{25,17},{10,2},{18,10},{26,18},{... | collective-permute-start | bytes 3080 | tf_op jit(solution)/shard_map/ppermute | solution.py:24
  71.0 5.9 %collective-permute-start.12 = (f32[1,1,1,2,128]{4,3,2,1,0:T(2,128)S(1)}, f32[1,1,1,2,128]{4,3,2,1,0:T(2,128)S(1)}, u32[]{:S(2)}, u32[]{:S(2)}) collective-permute-start(f32[1,1,1,2,128]{4,3,2,1,0:T(2,128)S(1)} %bitcast.160), channel_id=1, source_target_pairs={{0,8},{8,16},{16,24},{1,9},{9,17},{17,25},{2,10},{10,18},{18,26},{... | collective-permute-start | bytes 3080 | tf_op jit(solution)/shard_map/ppermute | solution.py:22
  77.0 5.8 %collective-permute-start.15 = (f32[1,3,1,2,128]{4,3,2,1,0:T(2,128)S(1)}, f32[1,3,1,2,128]{4,3,2,1,0:T(2,128)S(1)}, u32[]{:S(2)}, u32[]{:S(2)}) collective-permute-start(f32[1,3,1,2,128]{4,3,2,1,0:T(2,128)S(1)} %pad_maximum_fusion.20), channel_id=1, source_target_pairs={{4,0},{5,1},{6,2},{7,3},{12,8},{13,9},{14,10},{15,11},{20,16},{21,... | collective-permute-start | bytes 9224 | tf_op jit(solution)/shard_map/ppermute | solution.py:24
  78.3 5.9 %collective-permute-start.14 = (f32[1,3,1,2,128]{4,3,2,1,0:T(2,128)S(1)}, f32[1,3,1,2,128]{4,3,2,1,0:T(2,128)S(1)}, u32[]{:S(2)}, u32[]{:S(2)}) collective-permute-start(f32[1,3,1,2,128]{4,3,2,1,0:T(2,128)S(1)} %pad_maximum_fusion.20), channel_id=1, source_target_pairs={{0,4},{1,5},{2,6},{3,7},{8,12},{9,13},{10,14},{11,15},{16,20},{17,... | collective-permute-start | bytes 9224 | tf_op jit(solution)/shard_map/ppermute | solution.py:22
  84.1 2.8 %collective-permute-start.16 = (f32[1,3,3,1,128]{4,3,2,1,0:T(1,128)S(1)}, f32[1,3,3,1,128]{4,3,2,1,0:T(1,128)S(1)}, u32[]{:S(2)}, u32[]{:S(2)}) collective-permute-start(f32[1,3,3,1,128]{4,3,2,1,0:T(1,128)S(1)} %get-tuple-element.39), channel_id=1, source_target_pairs={{0,1},{1,2},{2,3},{4,5},{5,6},{6,7},{8,9},{9,10},{10,11},{12,13},{... | collective-permute-start | bytes 13832 | tf_op jit(solution)/shard_map/ppermute | solution.py:22
  85.6 6.6 %collective-permute-start.17 = (f32[1,3,3,1,128]{4,3,2,1,0:T(1,128)S(1)}, f32[1,3,3,1,128]{4,3,2,1,0:T(1,128)S(1)}, u32[]{:S(2)}, u32[]{:S(2)}) collective-permute-start(f32[1,3,3,1,128]{4,3,2,1,0:T(1,128)S(1)} %get-tuple-element.40), channel_id=1, source_target_pairs={{1,0},{2,1},{3,2},{5,4},{6,5},{7,6},{9,8},{10,9},{11,10},{13,12},{... | collective-permute-start | bytes 13832 | tf_op jit(solution)/shard_map/ppermute | solution.py:24
  132.8 18.7 %copy-start.8 = (f32[1,2,128]{2,1,0:T(2,128)}, f32[1,2,128]{2,1,0:T(2,128)S(1)}, u32[]{:S(2)}) copy-start(f32[1,2,128]{2,1,0:T(2,128)S(1)} %bitcast_divide_fusion.1) | copy-start | bytes 3076
  132.8 5.8 %collective-permute-start.19 = (f32[1,1,1,2,128]{4,3,2,1,0:T(2,128)S(1)}, f32[1,1,1,2,128]{4,3,2,1,0:T(2,128)S(1)}, u32[]{:S(2)}, u32[]{:S(2)}) collective-permute-start(f32[1,1,1,2,128]{4,3,2,1,0:T(2,128)S(1)} %bitcast.148), channel_id=1, source_target_pairs={{8,0},{16,8},{24,16},{9,1},{17,9},{25,17},{10,2},{18,10},{26,18},{... | collective-permute-start | bytes 3080 | tf_op jit(solution)/shard_map/ppermute | solution.py:24
  134.1 5.8 %collective-permute-start.18 = (f32[1,1,1,2,128]{4,3,2,1,0:T(2,128)S(1)}, f32[1,1,1,2,128]{4,3,2,1,0:T(2,128)S(1)}, u32[]{:S(2)}, u32[]{:S(2)}) collective-permute-start(f32[1,1,1,2,128]{4,3,2,1,0:T(2,128)S(1)} %bitcast.149), channel_id=1, source_target_pairs={{0,8},{8,16},{16,24},{1,9},{9,17},{17,25},{2,10},{10,18},{18,26},{... | collective-permute-start | bytes 3080 | tf_op jit(solution)/shard_map/ppermute | solution.py:22
  139.9 5.8 %collective-permute-start.21 = (f32[1,3,1,2,128]{4,3,2,1,0:T(2,128)S(1)}, f32[1,3,1,2,128]{4,3,2,1,0:T(2,128)S(1)}, u32[]{:S(2)}, u32[]{:S(2)}) collective-permute-start(f32[1,3,1,2,128]{4,3,2,1,0:T(2,128)S(1)} %pad_maximum_fusion.21), channel_id=1, source_target_pairs={{4,0},{5,1},{6,2},{7,3},{12,8},{13,9},{14,10},{15,11},{20,16},{21,... | collective-permute-start | bytes 9224 | tf_op jit(solution)/shard_map/ppermute | solution.py:24
  141.2 5.9 %collective-permute-start.20 = (f32[1,3,1,2,128]{4,3,2,1,0:T(2,128)S(1)}, f32[1,3,1,2,128]{4,3,2,1,0:T(2,128)S(1)}, u32[]{:S(2)}, u32[]{:S(2)}) collective-permute-start(f32[1,3,1,2,128]{4,3,2,1,0:T(2,128)S(1)} %pad_maximum_fusion.21), channel_id=1, source_target_pairs={{0,4},{1,5},{2,6},{3,7},{8,12},{9,13},{10,14},{11,15},{16,20},{17,... | collective-permute-start | bytes 9224 | tf_op jit(solution)/shard_map/ppermute | solution.py:22
  147.1 2.6 collective-permute-start.22
  148.4 3.1 %collective-permute-start.23 = (f32[1,3,3,1,128]{4,3,2,1,0:T(1,128)S(1)}, f32[1,3,3,1,128]{4,3,2,1,0:T(1,128)S(1)}, u32[]{:S(2)}, u32[]{:S(2)}) collective-permute-start(f32[1,3,3,1,128]{4,3,2,1,0:T(1,128)S(1)} %get-tuple-element.36), channel_id=1, source_target_pairs={{1,0},{2,1},{3,2},{5,4},{6,5},{7,6},{9,8},{10,9},{11,10},{13,12},{... | collective-permute-start | bytes 13832 | tf_op jit(solution)/shard_map/ppermute | solution.py:24
  193.1 14.3 %copy-start.15 = (f32[1,2,128]{2,1,0:T(2,128)}, f32[1,2,128]{2,1,0:T(2,128)S(1)}, u32[]{:S(2)}) copy-start(f32[1,2,128]{2,1,0:T(2,128)S(1)} %get-tuple-element.12) | copy-start | bytes 3076
  193.1 5.8 %collective-permute-start.25 = (f32[1,1,1,2,128]{4,3,2,1,0:T(2,128)S(1)}, f32[1,1,1,2,128]{4,3,2,1,0:T(2,128)S(1)}, u32[]{:S(2)}, u32[]{:S(2)}) collective-permute-start(f32[1,1,1,2,128]{4,3,2,1,0:T(2,128)S(1)} %bitcast.154), channel_id=1, source_target_pairs={{8,0},{16,8},{24,16},{9,1},{17,9},{25,17},{10,2},{18,10},{26,18},{... | collective-permute-start | bytes 3080 | tf_op jit(solution)/shard_map/ppermute | solution.py:24
  194.4 5.8 %collective-permute-start.24 = (f32[1,1,1,2,128]{4,3,2,1,0:T(2,128)S(1)}, f32[1,1,1,2,128]{4,3,2,1,0:T(2,128)S(1)}, u32[]{:S(2)}, u32[]{:S(2)}) collective-permute-start(f32[1,1,1,2,128]{4,3,2,1,0:T(2,128)S(1)} %bitcast.155), channel_id=1, source_target_pairs={{0,8},{8,16},{16,24},{1,9},{9,17},{17,25},{2,10},{10,18},{18,26},{... | collective-permute-start | bytes 3080 | tf_op jit(solution)/shard_map/ppermute | solution.py:22
  199.0 10.9 %copy-start.31 = (f32[1,1,1,2,128]{4,3,2,1,0:T(2,128)}, f32[1,1,1,2,128]{4,3,2,1,0:T(2,128)S(1)}, u32[]{:S(2)}) copy-start(f32[1,1,1,2,128]{4,3,2,1,0:T(2,128)S(1)} %collective-permute-done.25) | copy-start | bytes 3076
  200.3 9.6 %copy-start.32 = (f32[1,1,1,2,128]{4,3,2,1,0:T(2,128)}, f32[1,1,1,2,128]{4,3,2,1,0:T(2,128)S(1)}, u32[]{:S(2)}) copy-start(f32[1,1,1,2,128]{4,3,2,1,0:T(2,128)S(1)} %collective-permute-done.24) | copy-start | bytes 3076
  200.3 5.8 %collective-permute-start.27 = (f32[1,3,1,2,128]{4,3,2,1,0:T(2,128)S(1)}, f32[1,3,1,2,128]{4,3,2,1,0:T(2,128)S(1)}, u32[]{:S(2)}, u32[]{:S(2)}) collective-permute-start(f32[1,3,1,2,128]{4,3,2,1,0:T(2,128)S(1)} %pad_maximum_fusion.22), channel_id=1, source_target_pairs={{4,0},{5,1},{6,2},{7,3},{12,8},{13,9},{14,10},{15,11},{20,16},{21,... | collective-permute-start | bytes 9224 | tf_op jit(solution)/shard_map/ppermute | solution.py:24
  201.6 5.9 %collective-permute-start.26 = (f32[1,3,1,2,128]{4,3,2,1,0:T(2,128)S(1)}, f32[1,3,1,2,128]{4,3,2,1,0:T(2,128)S(1)}, u32[]{:S(2)}, u32[]{:S(2)}) collective-permute-start(f32[1,3,1,2,128]{4,3,2,1,0:T(2,128)S(1)} %pad_maximum_fusion.22), channel_id=1, source_target_pairs={{0,4},{1,5},{2,6},{3,7},{8,12},{9,13},{10,14},{11,15},{16,20},{17,... | collective-permute-start | bytes 9224 | tf_op jit(solution)/shard_map/ppermute | solution.py:22
  208.0 8.5 %collective-permute-start.28 = (f32[1,3,3,1,128]{4,3,2,1,0:T(1,128)}, f32[1,3,3,1,128]{4,3,2,1,0:T(1,128)}, u32[]{:S(2)}, u32[]{:S(2)}) collective-permute-start(f32[1,3,3,1,128]{4,3,2,1,0:T(1,128)} %get-tuple-element.31), channel_id=1, source_target_pairs={{0,1},{1,2},{2,3},{4,5},{5,6},{6,7},{8,9},{9,10},{10,11},{12,13},{... | collective-permute-start | bytes 13832 | tf_op jit(solution)/shard_map/ppermute | solution.py:22
  209.9 6.7 %collective-permute-start.29 = (f32[1,3,3,1,128]{4,3,2,1,0:T(1,128)}, f32[1,3,3,1,128]{4,3,2,1,0:T(1,128)}, u32[]{:S(2)}, u32[]{:S(2)}) collective-permute-start(f32[1,3,3,1,128]{4,3,2,1,0:T(1,128)} %get-tuple-element.32), channel_id=1, source_target_pairs={{1,0},{2,1},{3,2},{5,4},{6,5},{7,6},{9,8},{10,9},{11,10},{13,12},{... | collective-permute-start | bytes 13832 | tf_op jit(solution)/shard_map/ppermute | solution.py:24
  222.9 40.4 %copy-start.4 = (f32[3,2,128]{2,1,0:T(2,128)S(1)}, f32[3,2,128]{2,1,0:T(2,128)}, u32[]{:S(2)}) copy-start(f32[3,2,128]{2,1,0:T(2,128)} %copy-done.3) | copy-start | bytes 9220
  222.9 40.4 %copy-start.7 = (f32[2,128]{1,0:T(2,128)S(1)}, f32[2,128]{1,0:T(2,128)}, u32[]{:S(2)}) copy-start(f32[2,128]{1,0:T(2,128)} %copy-done.5) | copy-start | bytes 3076
  222.9 40.4 %copy-start.11 = (f32[3,1,1,2,128]{4,3,2,1,0:T(2,128)S(1)}, f32[3,1,1,2,128]{4,3,2,1,0:T(2,128)}, u32[]{:S(2)}) copy-start(f32[3,1,1,2,128]{4,3,2,1,0:T(2,128)} %param.4) | copy-start | bytes 9220
  222.9 40.4 %copy-start.14 = (f32[6,2,128]{2,1,0:T(2,128)S(1)}, f32[6,2,128]{2,1,0:T(2,128)}, u32[]{:S(2)}) copy-start(f32[6,2,128]{2,1,0:T(2,128)} %copy-done.12) | copy-start | bytes 18436
  223.0 40.4 %copy-start.25 = (f32[3,2]{1,0:T(4,128)S(1)}, f32[3,2]{1,0:T(4,128)}, u32[]{:S(2)}) copy-start(f32[3,2]{1,0:T(4,128)} %copy.31) | copy-start | bytes 76
  (19 other events, 45.6 us)
